TPU v7x, 512 devices: a whole 4x8x8 slice. The times are simulated.
512 devices in a mesh: group: 64 (over z, y), mp: 8 (over x, core).
Axes of the slice: x: 4, y: 8, z: 8, core: 2. Of those that a mesh axis runs over, the one named last changes fastest.
Arguments:
- tokens: bfloat16 [8192, 4096], P('group', 'mp'), may hold values from -3000 to 3000
- attn_gain: float32 [4096], replicated, may hold values from 0.1 to 1.9
- q_weight: bfloat16 [4096, 4096], P('group', 'mp'), may hold values from -0.09375 to 0.09375
- k_weight: bfloat16 [4096, 512], P('group'), may hold values from -0.09375 to 0.09375
- v_weight: bfloat16 [4096, 512], P('group'), may hold values from -0.09375 to 0.09375
- kv_pool: bfloat16 [4096, 8, 2, 16, 128], P('group', 'mp'), may hold values from -1000 to 1000
- page_table: int32 [256, 16], replicated, may hold values from 0 to 4095, as said below
- lengths: int32 [256], P('group'), may hold values from 2 to 256
- token_request: int32 [8192], P('group'), may hold values from 0 to 3
Outputs:
- attention: bfloat16 [8192, 4096], P('group', 'mp')
- decode_cache: bfloat16 [256, 8, 2, 256, 128], P('group', 'mp')
Inputs may be any that keep to these rules, and one draw needn't show every extreme that they name: Every pool page stands in exactly one slot of page_table. The pages that one group index holds for the requests of one owner (requests o * 4 to (o + 1) * 4 - 1) number at most 2, and exactly 2 for some pairs of holder and owner.
All inputs are finite; a program needn't handle non-finite values.
Results may differ from a plain program's by a relative error of at most 0.038.
Values may be sent and summed in bfloat16 or wider, within the bound.
No kernel may reach another device: no remote copies, remote signals or barrier semaphores. Data moves between devices by JAX's collectives and lax.ppermute only.
A program may use at most 64 MiB of HBM per device.

v0:
```python
import jax
import jax.numpy as jnp
from jax import lax
from jax.sharding import PartitionSpec as P

HEADS = 32
KVH = 4
rope_theta = 5000000.0
norm_eps = 1e-05


def from_partner(x, axis, bit):
    return lax.ppermute(x, axis, [(i, i ^ 1 << bit) for i in range(lax.axis_size(axis))])


def rotate(vectors, position):
    half_dim = vectors.shape[-1] // 2
    frequency = rope_theta ** (-(jnp.arange(half_dim, dtype=jnp.float32) / half_dim))
    angles = position.astype(jnp.float32)[:, None, None] * frequency[None, None, :]
    cosine = jnp.cos(angles)
    sine_part = jnp.sin(angles)
    first_half = vectors[..., :half_dim]
    second = vectors[..., half_dim:]
    return jnp.concatenate(
        [first_half * cosine - second * sine_part, second * cosine + first_half * sine_part],
        axis=-1,
    )


def normalize(group_rows, attn_gain):
    features = group_rows.astype(jnp.float32)
    root_mean = jnp.sqrt(jnp.mean(features * features, axis=-1, keepdims=True) + norm_eps)
    return (features / root_mean * attn_gain).astype(jnp.bfloat16)


def token_positions(token_request, group_lengths, request_count):
    member = (token_request[:, None] == jnp.arange(request_count, dtype=jnp.int32)[None, :]).astype(
        jnp.int32
    )
    earlier = jnp.sum((jnp.cumsum(member, axis=0) - member) * member, axis=1)
    return jnp.sum(member * group_lengths[None, :], axis=1) + earlier


def build_mask(token_request, group_lengths, max_len):
    request_count = group_lengths.shape[0]
    key_index = jnp.arange(request_count * max_len, dtype=jnp.int32)
    key_request = key_index // max_len
    key_alive = key_index % max_len < group_lengths[key_request]
    cached = (token_request[:, None] == key_request[None, :]) & key_alive[None, :]
    token_order = jnp.arange(token_request.shape[0], dtype=jnp.int32)
    fresh = (token_request[:, None] == token_request[None, :]) & (
        token_order[None, :] <= token_order[:, None]
    )
    return jnp.concatenate([cached, fresh], axis=1)


def weigh(scores, allowed):
    masked = jnp.where(allowed, scores, -1e30)
    row_top = jnp.max(masked, axis=-1, keepdims=True)
    exponent = jnp.exp(masked - row_top)
    return (exponent / jnp.sum(exponent, axis=-1, keepdims=True)).astype(jnp.bfloat16)


def on_device(
    tokens, attn_gain, q_weight, k_weight, v_weight, kv_pool, page_table, lengths, token_request
):
    groups = lax.axis_size("group")
    group_idx = lax.axis_index("group")
    mp_idx = lax.axis_index("mp")
    pool_pages = kv_pool.shape[0]
    pair_count = kv_pool.shape[1]
    page_len = kv_pool.shape[3]
    head_dim = kv_pool.shape[4]
    requests_here = lengths.shape[0]
    slot_count = pool_pages // requests_here
    max_len = slot_count * page_len
    capacity = 2 * pool_pages // groups
    flat_table = page_table.reshape(-1)
    slot_ids = jnp.arange(flat_table.shape[0], dtype=jnp.int32)
    owner_slot = jnp.zeros((flat_table.shape[0],), jnp.int32).at[flat_table].set(slot_ids)
    held_slots = lax.dynamic_slice_in_dim(owner_slot, group_idx * pool_pages, pool_pages)
    target_owner = held_slots // pool_pages
    slot_local = held_slots % pool_pages
    owner_hits = (target_owner[:, None] == jnp.arange(groups, dtype=jnp.int32)[None, :]).astype(
        jnp.int32
    )
    order_within = jnp.sum((jnp.cumsum(owner_hits, axis=0) - owner_hits) * owner_hits, axis=1)
    buffer_row = target_owner * capacity + order_within
    page_rows = kv_pool.reshape(pool_pages, -1)
    row_width = page_rows.shape[1]
    outgoing = (
        jnp.zeros((groups * capacity, row_width), jnp.bfloat16)
        .at[buffer_row]
        .set(page_rows)
        .reshape(groups, capacity, row_width)
    )
    outgoing_slots = (
        jnp.full((groups * capacity,), -1, jnp.int32)
        .at[buffer_row]
        .set(slot_local)
        .reshape(groups, capacity)
    )
    arrived, arrived_slots = (
        lax.all_to_all(outgoing, "group", split_axis=0, concat_axis=0, tiled=True),
        lax.all_to_all(outgoing_slots, "group", split_axis=0, concat_axis=0, tiled=True),
    )
    landing = jnp.where(arrived_slots < 0, pool_pages, arrived_slots).reshape(-1)
    placed = (
        jnp.zeros((pool_pages + 1, row_width), jnp.bfloat16)
        .at[landing]
        .set(arrived.reshape(-1, row_width))[:pool_pages]
    )
    decoded = placed.reshape(requests_here, slot_count, pair_count, 2, page_len, head_dim)
    decoded = decoded.transpose(0, 2, 3, 1, 4, 5).reshape(
        requests_here, pair_count, 2, max_len, head_dim
    )
    alive_mask = jnp.arange(max_len, dtype=jnp.int32)[None, :] < lengths[:, None]
    decoded = jnp.where(alive_mask[:, None, None, :, None], decoded, jnp.zeros((), jnp.bfloat16))
    whole_rows = lax.all_gather(tokens, "mp", axis=1, tiled=True)
    normed = normalize(whole_rows, attn_gain)
    rows_here = tokens.shape[0]
    heads_here = q_weight.shape[1] // head_dim
    per_kv = HEADS // KVH
    first_kv = mp_idx * heads_here // per_kv
    key_cols = lax.dynamic_slice_in_dim(k_weight, first_kv * head_dim, head_dim, 1)
    value_cols = lax.dynamic_slice_in_dim(v_weight, first_kv * head_dim, head_dim, 1)
    query_sum = jnp.dot(
        normed,
        lax.all_gather(q_weight, "group", axis=0, tiled=True),
        preferred_element_type=jnp.float32,
    )
    key_sum = jnp.dot(
        normed,
        lax.all_gather(key_cols, "group", axis=0, tiled=True),
        preferred_element_type=jnp.float32,
    )
    value_sum = jnp.dot(
        normed,
        lax.all_gather(value_cols, "group", axis=0, tiled=True),
        preferred_element_type=jnp.float32,
    )
    position = token_positions(token_request, lengths, requests_here)
    queries = (
        rotate(query_sum.reshape(rows_here, heads_here, head_dim), position)
        .astype(jnp.bfloat16)
        .transpose(1, 0, 2)
    )
    new_keys = rotate(key_sum.reshape(rows_here, 1, head_dim), position).astype(jnp.bfloat16)[:, 0]
    new_values = value_sum.astype(jnp.bfloat16)
    allowed = build_mask(token_request, lengths, max_len)
    score_scale = head_dim ** (-0.5)
    partner_cache = from_partner(decoded, "mp", 0)
    is_even = mp_idx % 2 == 0
    layer_zero = jnp.where(is_even, decoded, partner_cache)[:, 0]
    all_keys = jnp.concatenate(
        [layer_zero[:, 0].reshape(requests_here * max_len, head_dim), new_keys], axis=0
    )
    all_values = jnp.concatenate(
        [layer_zero[:, 1].reshape(requests_here * max_len, head_dim), new_values], axis=0
    )

    def attend(query_one):
        scores = (
            jnp.einsum("td,nd->tn", query_one, all_keys, preferred_element_type=jnp.float32)
            * score_scale
        )
        attn_probs = weigh(scores, allowed)
        return jnp.dot(attn_probs, all_values, preferred_element_type=jnp.float32).astype(
            jnp.bfloat16
        )

    heads_out = lax.map(attend, queries)
    attention = heads_out.transpose(1, 0, 2).reshape(rows_here, heads_here * head_dim)
    return (attention, partner_cache)


def solution(mesh):
    return jax.shard_map(
        on_device,
        mesh=mesh,
        in_specs=(
            P("group", "mp"),
            P(),
            P("group", "mp"),
            P("group", None),
            P("group", None),
            P("group", "mp", None, None, None),
            P(),
            P("group"),
            P("group"),
        ),
        out_specs=(P("group", "mp"), P("group", "mp", None, None, None)),
        check_vma=False,
    )
```

profile of v0, /device:TPU:2, one launch (start us, length us, event | category | flops | bytes accessed | tf_op | source)
XLA Modules:
  0.0 325.8 jit_solution(18150802313634479583)
XLA Ops:
  8.7 1.3 constant_dynamic-slice_fusion
  10.6 0.8 copy.29
  11.6 15.5 %scatter_custom_fusion = s32[4096]{0:T(1024)S(1)} fusion(s32[4096]{0:T(1024)S(1)} %bitcast.75, s32[4096]{0:T(1024)S(1)} %iota.46, s32[]{:T(128)} %copy.64), kind=kCustom, calls=%fused_computation.79 | custom fusion | bytes 16388 | tf_op jit(solution)/shard_map/scatter | solution.py:80
  29.2 16.6 %all-to-all-start = ((s32[64,1,2]{2,1,0:T(1,128)}), s32[64,1,2]{2,1,0:T(1,128)S(1)}, u32[]{:S(2)}, u32[]{:S(2)}) async-start(s32[64,1,2]{2,1,0:T(1,128)} %bitcast.4), calls=%async_computation | async-start | bytes 65536 | tf_op jit(solution)/shard_map/all_to_all | solution.py:105
  46.8 1.5 fusion.45
  48.2 2.6 compare_select_fusion.2
  50.8 0.9 select_reduce_fusion
  51.7 0.8 fusion.17
  53.5 2.3 scatter_custom_fusion.2
  55.8 1.5 reshape.342
  57.8 12.4 %all-to-all-start.1 = ((bf16[64,2,4096]{2,1,0:T(2,128)(2,1)}), bf16[64,2,4096]{2,1,0:T(2,128)(2,1)S(1)}, u32[]{:S(2)}, u32[]{:S(2)}) async-start(bf16[64,2,4096]{2,1,0:T(2,128)(2,1)} %reshape.342), calls=%async_computation.1 | async-start | bytes 2097152 | tf_op jit(solution)/shard_map/all_to_all | solution.py:104
  71.8 1.5 fusion.7
  73.4 1.6 fusion.9
  74.9 24.7 %all-to-all-done.1 = bf16[64,2,4096]{2,1,0:T(2,128)(2,1)S(1)} async-done(((bf16[64,2,4096]{2,1,0:T(2,128)(2,1)}), bf16[64,2,4096]{2,1,0:T(2,128)(2,1)S(1)}, u32[]{:S(2)}, u32[]{:S(2)}) %all-to-all-start.1) | async-done | bytes 1048608 | tf_op jit(solution)/shard_map/all_to_all | solution.py:104
  99.7 1.2 reshape.387
  100.9 2.8 scatter_custom_fusion.3
  104.1 2.1 collective-permute-start
  106.2 35.6 %all-gather.9.cloned.1.call-done = bf16[4096,128]{1,0:T(8,128)(2,1)} async-done(((bf16[64,128]{1,0:T(8,128)(2,1)}), bf16[4096,128]{1,0:T(8,128)(2,1)}) %all-gather.9.cloned.1.call-update) | async-done | bytes 1048592 | tf_op jit(solution)/shard_map/all_gather | solution.py:134
  141.8 1.7 convolution_bitcast_fusion
  143.9 80.1 %all-gather.11.cloned.1.call-done = bf16[4096,128]{1,0:T(8,128)(2,1)} async-done(((bf16[64,128]{1,0:T(8,128)(2,1)}), bf16[4096,128]{1,0:T(8,128)(2,1)}) %all-gather.11.cloned.1.call-update) | async-done | bytes 1048592 | tf_op jit(solution)/shard_map/all_gather | solution.py:139
  224.0 1.6 convolution_convert_fusion.1
  226.0 84.7 %all-gather.7.cloned.1.call-done = bf16[4096,512]{1,0:T(8,128)(2,1)} async-done(((bf16[64,512]{1,0:T(8,128)(2,1)}), bf16[4096,512]{1,0:T(8,128)(2,1)}) %all-gather.7.cloned.1.call-update) | async-done | bytes 4194320 | tf_op jit(solution)/shard_map/all_gather | solution.py:129
  310.6 2.9 fusion.46
  314.1 3.8 %while.10 = (s32[]{:T(128)}, bf16[4,128,128]{2,1,0:T(8,128)(2,1)S(1)}, bf16[4,128,128]{2,1,0:T(8,128)(2,1)S(1)}, bf16[1152,128]{1,0:T(8,128)(2,1)S(1)}, pred[128...) while((s32[]{:T(128)}, bf16[4,128,128]{2,1,0:T(8,128)(2,1)S(1)}, ...), condition=%wide.region_13.14_spmd, body=%wide.region_10.13_spmd.sunk | while | flops 76693248 | bytes 2574941 | solution.py:172
  (74 shorter events, 14.8 us)
Async XLA Ops:
  7.2 0.8 copy-start
  7.2 64.6 %all-gather.5.cloned.1.call-start = ((), (), s32[]{:S(2)}) async-start(), calls=%async_computation.2 | async-start | bytes 1179648 | tf_op jit(solution)/shard_map/all_gather | solution.py:119
  7.9 133.9 %all-gather.9.cloned.1.call-start = ((), (), s32[]{:S(2)}) async-start(), calls=%async_computation.4 | async-start | bytes 1064960 | tf_op jit(solution)/shard_map/all_gather | solution.py:134
  8.7 215.3 %all-gather.11.cloned.1.call-start = ((), (), s32[]{:S(2)}) async-start(), calls=%async_computation.5 | async-start | bytes 1064960 | tf_op jit(solution)/shard_map/all_gather | solution.py:139
  10.1 300.6 %all-gather.7.cloned.1.call-start = ((), (), s32[]{:S(2)}) async-start(), calls=%async_computation.3 | async-start | bytes 4259840 | tf_op jit(solution)/shard_map/all_gather | solution.py:129
  29.2 28.5 %all-to-all-start = ((s32[64,1,2]{2,1,0:T(1,128)}), s32[64,1,2]{2,1,0:T(1,128)S(1)}, u32[]{:S(2)}, u32[]{:S(2)}) async-start(s32[64,1,2]{2,1,0:T(1,128)} %bitcast.4), calls=%async_computation | async-start | bytes 65536 | tf_op jit(solution)/shard_map/all_to_all | solution.py:105
  55.8 14.4 %copy-start.2 = (s32[128]{0:T(128)S(1)}, s32[128]{0:T(128)}, u32[]{:S(2)}) copy-start(s32[128]{0:T(128)} %param.19) | copy-start | bytes 1540
  57.3 16.0 %copy-start.1 = (f32[4096]{0:T(1024)S(1)}, f32[4096]{0:T(1024)}, u32[]{:S(2)}) copy-start(f32[4096]{0:T(1024)} %param.12) | copy-start | bytes 49156
  57.8 41.9 %all-to-all-start.1 = ((bf16[64,2,4096]{2,1,0:T(2,128)(2,1)}), bf16[64,2,4096]{2,1,0:T(2,128)(2,1)S(1)}, u32[]{:S(2)}, u32[]{:S(2)}) async-start(bf16[64,2,4096]{2,1,0:T(2,128)(2,1)} %reshape.342), calls=%async_computation.1 | async-start | bytes 2097152 | tf_op jit(solution)/shard_map/all_to_all | solution.py:104
  104.1 121.5 %collective-permute-start = (bf16[4,1,2,256,128]{4,3,2,0,1:T(8,128)(2,1)S(1)}, bf16[4,1,2,256,128]{4,3,2,0,1:T(8,128)(2,1)S(1)}, u32[]{:S(2)}, u32[]{:S(2)}) collective-permute-start(bf16[4,1,2,256,128]{4,3,2,0,1:T(8,128)(2,1)S(1)} %bitcast_select_fusion), channel_id=1, source_target_pairs={{0,1},{1,0},{2,3},{3,2},{4,5},{5,4},{6,7},{7,6},{8,9},{9,8},{10,11... | collective-permute-start | bytes 1572872 | tf_op jit(solution)/shard_map/ppermute | solution.py:13
Sparse Core Ops, SparseCore 0:
  10.1 31.9 all-gather.4
  45.7 96.0 all-gather.8
  144.9 79.0 all-gather.10
  226.9 83.6 all-gather.6
where the time goes:
time: 327 us; the launch traced here: 326 us
  waiting for transfers between devices  227 us (69%)
  local copies, waits for them, and re-layouts  32 us (10%)
  starting transfers between devices  31.2 us (10%)
  between operations  14.2 us (4%)
  other arithmetic  12.5 us (4%)
  matrix products  8.96 us (3%)
    all_gather x1, waiting for transfers between devices, on_device(): lax.all_gather(q_weight, 'group', axis=0, tiled=True)  84.7 us
    all_gather x1, waiting for transfers between devices, on_device(): lax.all_gather(value_cols, 'group', axis=0, tiled=True)  80.1 us
    all_gather x1, waiting for transfers between devices, on_device(): lax.all_gather(key_cols, 'group', axis=0, tiled=True)  35.6 us
    all_to_all x1, waiting for transfers between devices, on_device(): lax.all_to_all(outgoing, 'group', split_axis=0, concat_axis=0, tiled=True)  24.7 us
    all_to_all x1, starting transfers between devices, on_device(): lax.all_to_all(outgoing_slots, 'group', split_axis=0, concat_axis=0, tile...  16.6 us
    scatter x1, local copies, waits for them, and re-layouts, on_device(): jnp.zeros((flat_table.shape[0],), jnp.int32).at[flat_table].set(slot_ids)  15.5 us
    all_to_all x1, starting transfers between devices, on_device(): lax.all_to_all(outgoing, 'group', split_axis=0, concat_axis=0, tiled=True)  12.4 us
  transfers between devices with their start and end apart: 7, of which 5 were waited for; matrix products, arithmetic and copies ran while one was open for 14% of the time, Pallas kernels for 0%

commit v1 on v0

--- a/solution.py
+++ b/solution.py
@@ -126,7 +126,9 @@
     value_cols = lax.dynamic_slice_in_dim(v_weight, first_kv * head_dim, head_dim, 1)
     query_sum = jnp.dot(
         normed,
-        lax.all_gather(q_weight, "group", axis=0, tiled=True),
+        jnp.concatenate(
+            lax.all_to_all(jnp.stack([q_weight] * lax.axis_size("group")), "group", 0, 0), axis=0
+        ),
         preferred_element_type=jnp.float32,
     )
     key_sum = jnp.dot(

time: 327 us -> 365 us (1.12)
  waiting for transfers between devices: 227 us -> 263 us
  local copies, waits for them, and re-layouts: 32 us -> 38.4 us
  other arithmetic: 12.5 us -> 8.07 us
    all_gather x1, waiting for transfers between devices: 35.6 us -> 145 us  [on_device(): lax.all_gather(key_cols, 'group', axis=0, tiled=True)]
    all_gather x1 -> x0, waiting for transfers between devices: 84.7 us -> none  [on_device(): lax.all_gather(q_weight, 'group', axis=0, tiled=True)]
    all_to_all x1, starting transfers between devices: 12.4 us -> 4.65 us  [on_device(): lax.all_to_all(outgoing, 'group', split_axis=0, concat_axis=0, tiled=True)]
    all_to_all x1, waiting for transfers between devices: 0.43 us -> 8.14 us  [on_device(): lax.all_to_all(outgoing_slots, 'group', split_axis=0, concat_axis=0, tile...]
    all_to_all x0 -> x1, starting transfers between devices: none -> 6.75 us  [on_device(): lax.all_to_all(jnp.stack([q_weight] * lax.axis_size('group')), 'group', 0...]
    dot_general x0 -> x1, local copies, waits for them, and re-layouts: none -> 6.46 us  [on_device(): jnp.dot(normed, jnp.concatenate(lax.all_to_all(jnp.stack([q_weight] * lax...]
    all_to_all x1, waiting for transfers between devices: 24.7 us -> 28.4 us  [on_device(): lax.all_to_all(outgoing, 'group', split_axis=0, concat_axis=0, tiled=True)]
  transfers between devices with their start and end apart: 7 -> 7, of which waited for: 5 -> 4; matrix products, arithmetic and copies ran while one was open for 14% -> 6% of each run, Pallas kernels for 0% -> 0%
where the time goes in v1:
time: 365 us; the launch traced here: 364 us
  waiting for transfers between devices  263 us (72%)
  local copies, waits for them, and re-layouts  38.4 us (11%)
  starting transfers between devices  30.2 us (8%)
  between operations  14.2 us (4%)
  matrix products  9.92 us (3%)
  other arithmetic  8.07 us (2%)
    all_gather x1, waiting for transfers between devices, on_device(): lax.all_gather(key_cols, 'group', axis=0, tiled=True)  145 us
    all_gather x1, waiting for transfers between devices, on_device(): lax.all_gather(value_cols, 'group', axis=0, tiled=True)  80.5 us
    all_to_all x1, waiting for transfers between devices, on_device(): lax.all_to_all(outgoing, 'group', split_axis=0, concat_axis=0, tiled=True)  28.4 us
    all_to_all x1, starting transfers between devices, on_device(): lax.all_to_all(outgoing_slots, 'group', split_axis=0, concat_axis=0, tile...  16.6 us
    scatter x1, local copies, waits for them, and re-layouts, on_device(): jnp.zeros((flat_table.shape[0],), jnp.int32).at[flat_table].set(slot_ids)  15.5 us
    all_to_all x1, waiting for transfers between devices, on_device(): lax.all_to_all(outgoing_slots, 'group', split_axis=0, concat_axis=0, tile...  8.14 us
  transfers between devices with their start and end apart: 7, of which 4 were waited for; matrix products, arithmetic and copies ran while one was open for 6% of the time, Pallas kernels for 0%

profile of v1, /device:TPU:2, one launch (start us, length us, event | category | flops | bytes accessed | tf_op | source)
XLA Modules:
  0.0 364.0 jit_solution(10445298972479548596)
XLA Ops:
  7.2 0.8 copy.28
  8.2 15.5 %scatter_custom_fusion = s32[4096]{0:T(1024)S(1)} fusion(s32[4096]{0:T(1024)S(1)} %bitcast.81, s32[4096]{0:T(1024)S(1)} %iota.46, s32[]{:T(128)} %copy.59), kind=kCustom, calls=%fused_computation.81 | custom fusion | bytes 16388 | tf_op jit(solution)/shard_map/scatter | solution.py:80
  24.3 0.8 scatter_custom_fusion.1
  25.8 16.6 %all-to-all-start.1 = ((s32[64,1,2]{2,1,0:T(1,128)}), s32[64,1,2]{2,1,0:T(1,128)S(1)}, u32[]{:S(2)}, u32[]{:S(2)}) async-start(s32[64,1,2]{2,1,0:T(1,128)} %bitcast.8), calls=%async_computation.1 | async-start | bytes 65536 | tf_op jit(solution)/shard_map/all_to_all | solution.py:105
  42.4 2.3 scatter_custom_fusion.2
  44.7 1.5 reshape.346
  46.2 8.1 %all-to-all-done.1 = s32[64,1,2]{2,1,0:T(1,128)S(1)} async-done(((s32[64,1,2]{2,1,0:T(1,128)}), s32[64,1,2]{2,1,0:T(1,128)S(1)}, u32[]{:S(2)}, u32[]{:S(2)}) %all-to-all-start.1) | async-done | bytes 544 | tf_op jit(solution)/shard_map/all_to_all | solution.py:105
  54.3 4.7 %all-to-all-start.2 = ((bf16[64,2,4096]{2,1,0:T(2,128)(2,1)}), bf16[64,2,4096]{2,1,0:T(2,128)(2,1)S(1)}, u32[]{:S(2)}, u32[]{:S(2)}) async-start(bf16[64,2,4096]{2,1,0:T(2,128)(2,1)} %reshape.346), calls=%async_computation.2 | async-start | bytes 2097152 | tf_op jit(solution)/shard_map/all_to_all | solution.py:104
  59.7 28.4 %all-to-all-done.2 = bf16[64,2,4096]{2,1,0:T(2,128)(2,1)S(1)} async-done(((bf16[64,2,4096]{2,1,0:T(2,128)(2,1)}), bf16[64,2,4096]{2,1,0:T(2,128)(2,1)S(1)}, u32[]{:S(2)}, u32[]{:S(2)}) %all-to-all-start.2) | async-done | bytes 1048608 | tf_op jit(solution)/shard_map/all_to_all | solution.py:104
  88.2 2.5 stack.2
  90.6 6.7 %all-to-all-start = ((bf16[64,64,512]{2,1,0:T(8,128)(2,1)}), bf16[64,64,512]{2,1,0:T(8,128)(2,1)}, u32[]{:S(2)}, u32[]{:S(2)}) async-start(bf16[64,64,512]{2,1,0:T(8,128)(2,1)} %stack.2), calls=%async_computation | async-start | bytes 8388608 | tf_op jit(solution)/shard_map/all_to_all | solution.py:130
  98.2 1.3 constant_dynamic-slice_fusion
  100.5 2.6 compare_select_fusion.2
  105.4 1.5 fusion.7
  107.3 2.1 scatter_custom_fusion.3
  109.9 2.1 collective-permute-start
  112.0 145.2 %all-gather.6.cloned.1.call-done = bf16[4096,128]{1,0:T(8,128)(2,1)} async-done(((bf16[64,128]{1,0:T(8,128)(2,1)}), bf16[4096,128]{1,0:T(8,128)(2,1)}) %all-gather.6.cloned.1.call-update) | async-done | bytes 1048592 | tf_op jit(solution)/shard_map/all_gather | solution.py:136
  257.2 1.9 convolution_bitcast_fusion
  259.4 80.5 %all-gather.8.cloned.1.call-done = bf16[4096,128]{1,0:T(8,128)(2,1)} async-done(((bf16[64,128]{1,0:T(8,128)(2,1)}), bf16[4096,128]{1,0:T(8,128)(2,1)}) %all-gather.8.cloned.1.call-update) | async-done | bytes 1048592 | tf_op jit(solution)/shard_map/all_gather | solution.py:141
  340.0 1.8 convolution_convert_fusion.1
  342.1 6.5 %copy.27 = bf16[512,4096]{1,0:T(8,128)(2,1)} copy(bf16[512,4096]{0,1:T(8,128)(2,1)} %bitcast.4) | data formatting | bytes 8388608 | tf_op jit(solution)/shard_map/dot_general | solution.py:127
  348.5 3.5 fusion.10
  352.1 3.9 %while.10 = (s32[]{:T(128)}, bf16[4,128,128]{2,1,0:T(8,128)(2,1)S(1)}, bf16[4,128,128]{1,2,0:T(8,128)(2,1)S(1)}, bf16[1152,128]{1,0:T(8,128)(2,1)S(1)}, pred[128...) while((s32[]{:T(128)}, bf16[4,128,128]{2,1,0:T(8,128)(2,1)S(1)}, ...), condition=%wide.region_13.14_spmd, body=%wide.region_10.13_spmd.sunk | while | flops 76693248 | bytes 2574941 | solution.py:174
  356.7 0.8 copy.60
  (78 shorter events, 12.0 us)
Async XLA Ops:
  7.2 90.3 %copy-start = (bf16[64,512]{1,0:T(8,128)(2,1)S(1)}, bf16[64,512]{1,0:T(8,128)(2,1)}, u32[]{:S(2)}) copy-start(bf16[64,512]{1,0:T(8,128)(2,1)} %param.14) | copy-start | bytes 196612
  25.8 28.5 %all-to-all-start.1 = ((s32[64,1,2]{2,1,0:T(1,128)}), s32[64,1,2]{2,1,0:T(1,128)S(1)}, u32[]{:S(2)}, u32[]{:S(2)}) async-start(s32[64,1,2]{2,1,0:T(1,128)} %bitcast.8), calls=%async_computation.1 | async-start | bytes 65536 | tf_op jit(solution)/shard_map/all_to_all | solution.py:105
  44.7 43.5 %copy-start.2 = (bf16[64,512]{1,0:T(8,128)(2,1)S(1)}, bf16[64,512]{1,0:T(8,128)(2,1)}, u32[]{:S(2)}) copy-start(bf16[64,512]{1,0:T(8,128)(2,1)} %param.13) | copy-start | bytes 196612
  54.3 33.8 %all-to-all-start.2 = ((bf16[64,2,4096]{2,1,0:T(2,128)(2,1)}), bf16[64,2,4096]{2,1,0:T(2,128)(2,1)S(1)}, u32[]{:S(2)}, u32[]{:S(2)}) async-start(bf16[64,2,4096]{2,1,0:T(2,128)(2,1)} %reshape.346), calls=%async_computation.2 | async-start | bytes 2097152 | tf_op jit(solution)/shard_map/all_to_all | solution.py:104
  59.0 46.4 %all-gather.4.cloned.1.call-start = ((), (), s32[]{:S(2)}) async-start(), calls=%async_computation.3 | async-start | bytes 1179648 | tf_op jit(solution)/shard_map/all_gather | solution.py:119
  90.6 8.9 %copy-start.3 = (s32[128]{0:T(128)S(1)}, s32[128]{0:T(128)}, u32[]{:S(2)}) copy-start(s32[128]{0:T(128)} %param.19) | copy-start | bytes 1540
  90.6 9.2 %copy-start.4 = (s32[4]{0:T(128)S(1)}, s32[4]{0:T(128)}, u32[]{:S(2)}) copy-start(s32[4]{0:T(128)} %param.18) | copy-start | bytes 52
  90.6 251.4 %all-to-all-start = ((bf16[64,64,512]{2,1,0:T(8,128)(2,1)}), bf16[64,64,512]{2,1,0:T(8,128)(2,1)}, u32[]{:S(2)}, u32[]{:S(2)}) async-start(bf16[64,64,512]{2,1,0:T(8,128)(2,1)} %stack.2), calls=%async_computation | async-start | bytes 8388608 | tf_op jit(solution)/shard_map/all_to_all | solution.py:130
  97.4 159.8 %all-gather.6.cloned.1.call-start = ((), (), s32[]{:S(2)}) async-start(), calls=%async_computation.4 | async-start | bytes 1064960 | tf_op jit(solution)/shard_map/all_gather | solution.py:136
  98.1 241.8 %all-gather.8.cloned.1.call-start = ((), (), s32[]{:S(2)}) async-start(), calls=%async_computation.5 | async-start | bytes 1064960 | tf_op jit(solution)/shard_map/all_gather | solution.py:141
  109.5 147.8 %copy-start.1 = (bf16[128,4096]{1,0:T(8,128)(2,1)S(1)}, bf16[128,4096]{1,0:T(8,128)(2,1)}, u32[]{:S(2)}) copy-start(bf16[128,4096]{1,0:T(8,128)(2,1)} %all-gather.4.cloned.1.call-done) | copy-start | bytes 3145732
  109.5 147.8 %copy-start.5 = (f32[4096]{0:T(1024)S(1)}, f32[4096]{0:T(1024)}, u32[]{:S(2)}) copy-start(f32[4096]{0:T(1024)} %param.12) | copy-start | bytes 49156
  109.9 231.9 %collective-permute-start = (bf16[4,1,2,256,128]{4,3,2,0,1:T(8,128)(2,1)S(1)}, bf16[4,1,2,256,128]{4,3,2,0,1:T(8,128)(2,1)S(1)}, u32[]{:S(2)}, u32[]{:S(2)}) collective-permute-start(bf16[4,1,2,256,128]{4,3,2,0,1:T(8,128)(2,1)S(1)} %bitcast_select_fusion), channel_id=1, source_target_pairs={{0,1},{1,0},{2,3},{3,2},{4,5},{5,4},{6,7},{7,6},{8,9},{9,8},{10,11... | collective-permute-start | bytes 1572872 | tf_op jit(solution)/shard_map/ppermute | solution.py:13
Sparse Core Ops, SparseCore 0:
  61.9 28.1 all-gather.3
  101.8 155.3 all-gather.5
  260.9 79.0 all-gather.7
